TPU v7x, 128 devices: a whole 4x4x4 slice. The times are simulated.
128 devices in a mesh: layer: 16 (over y, x), prow: 4 (over z), pcol: 2 (over core).
Axes of the slice: x: 4, y: 4, z: 4, core: 2. Of those that a mesh axis runs over, the one named last changes fastest.
Arguments:
- front: bfloat16 [16, 2048, 32768], P('layer', 'prow', 'pcol'), may hold values from -6 to 6
- pivots: bfloat16 [16, 2, 256, 32768], P('layer', None, 'prow', 'pcol'), may hold values from -0.8984375 to 0.8984375
- inverses: bfloat16 [16, 2, 256, 256], P('layer'), may hold values from -0.1875 to 0.1875
- slab_pattern: int32 [16, 8, 128], P('layer', 'prow', 'pcol'), may hold values 0 or 1
- pivot_pattern: int32 [16, 2, 128], P('layer', None, 'pcol'), may hold values from 0 to 1, as said below
Outputs:
- ancestor: float32 [4, 16, 32, 32768], P('prow', 'layer', None, 'pcol')
- lower: bfloat16 [16, 2048, 512], P('layer', 'prow')
- upper: bfloat16 [16, 256, 32768], P('layer', 'prow', 'pcol')
Inputs may be any that keep to these rules, and one draw needn't show every extreme that they name: `pivot_pattern`: each entry says whether that block of the pivot rows is structurally nonzero. `slab_pattern`: each entry says whether that block of the front rows is structurally nonzero.
All inputs are finite; a program needn't handle non-finite values.
Results may differ from a plain program's by a relative error of at most 0.014.
Values may be sent and summed in bfloat16 or wider, within the bound.
No kernel may reach another device: no remote copies, remote signals or barrier semaphores. Data moves between devices by JAX's collectives and lax.ppermute only.
A program may use at most 192 MiB of HBM per device.

v0:
```python
import jax
import jax.numpy as jnp
from jax import lax
from jax.sharding import PartitionSpec as P


def spread(value, axis, root):
    mine = lax.axis_index(axis) == root
    return lax.psum(jnp.where(mine, value, jnp.zeros_like(value)), axis)


def on_device(front, pivots, inverses, slab_pattern, pivot_pattern):
    block_size = inverses.shape[-1]
    panel_width = 2 * block_size
    row_count = front.shape[1]
    col_count = front.shape[2]
    own_rows = pivots.shape[2]
    masked = (
        front[0].reshape(row_count // block_size, block_size, col_count // block_size, block_size)
        * slab_pattern[0].astype(jnp.bfloat16)[:, None, :, None]
    ).reshape(row_count, col_count)
    pivot_masked = (
        pivots[0].reshape(2, own_rows, col_count // block_size, block_size)
        * pivot_pattern[0].astype(jnp.bfloat16)[:, None, :, None]
    ).reshape(2, own_rows, col_count)
    first_inverse = inverses[0, 0]
    second_inverse = inverses[0, 1]
    row_offset = lax.axis_index("prow") * own_rows
    gathered = lax.all_gather(pivot_masked, "prow", axis=1, tiled=True)
    panel_cols = spread(
        jnp.concatenate(
            [masked[:, :panel_width], gathered[0][:, :panel_width], gathered[1][:, :panel_width]], 0
        ),
        "pcol",
        0,
    )
    front_cols = panel_cols[:row_count]
    pivot_cols = panel_cols[row_count : row_count + block_size]
    second_cols = panel_cols[row_count + block_size :]
    lower_pivot = jnp.dot(
        second_cols[:, :block_size], first_inverse, preferred_element_type=jnp.float32
    ).astype(jnp.bfloat16)
    upper_first = gathered[0]
    upper_second = (
        gathered[1].astype(jnp.float32)
        - jnp.dot(lower_pivot, upper_first, preferred_element_type=jnp.float32)
    ).astype(jnp.bfloat16)
    upper_own = lax.dynamic_slice_in_dim(upper_second, row_offset, own_rows, 0)
    lower_first = jnp.dot(
        front_cols[:, :block_size], first_inverse, preferred_element_type=jnp.float32
    ).astype(jnp.bfloat16)
    carried = (
        front_cols[:, block_size:].astype(jnp.float32)
        - jnp.dot(
            lower_first, pivot_cols[:, block_size:panel_width], preferred_element_type=jnp.float32
        )
    ).astype(jnp.bfloat16)
    lower_second = jnp.dot(carried, second_inverse, preferred_element_type=jnp.float32).astype(
        jnp.bfloat16
    )
    lower_panel = jnp.concatenate([lower_first, lower_second], 1)
    stacked = jnp.concatenate([upper_first, upper_second], 0)
    col_index = lax.axis_index("pcol") * col_count + jnp.arange(col_count, dtype=jnp.int32)
    retained = col_index >= panel_width
    schur_rows = masked.astype(jnp.float32) - jnp.dot(
        lower_panel, stacked, preferred_element_type=jnp.float32
    )
    schur_rows = jnp.where(retained[None, :], schur_rows, jnp.zeros_like(schur_rows))
    summed = lax.psum_scatter(
        schur_rows.astype(jnp.bfloat16), "layer", scatter_dimension=0, tiled=True
    ).astype(jnp.float32)
    ancestor = summed.reshape(1, 1, summed.shape[0], col_count)
    return (ancestor, lower_panel[None], upper_own[None])


def solution(mesh):
    placed = (
        P("layer", "prow", "pcol"),
        P("layer", None, "prow", "pcol"),
        P("layer", None, None, None),
        P("layer", "prow", "pcol"),
        P("layer", None, "pcol"),
    )
    return jax.shard_map(
        on_device,
        mesh=mesh,
        in_specs=placed,
        out_specs=(
            P("prow", "layer", None, "pcol"),
            P("layer", "prow", None),
            P("layer", "prow", "pcol"),
        ),
        check_vma=False,
    )
```

profile of v0, /device:TPU:1, one launch (start us, length us, event | category | flops | bytes accessed | tf_op | source)
XLA Modules:
  0.0 362.8 jit_solution(13036660158709411677)
XLA Ops:
  7.2 0.0 all-gather.2.cloned.1.call-start
  7.2 0.7 convert_bitcast_fusion
  7.9 0.1 broadcast_bitcast_fusion
  8.0 0.1 copy.10
  8.1 4.8 %bitcast_multiply_fusion.1 = bf16[2,64,16384]{2,1,0:T(8,128)(2,1)} fusion(bf16[1,2,64,16384]{3,2,1,0:T(8,128)(2,1)} %param.6, bf16[2,16384]{1,0:T(2,128)(2,1)S(1)} %bitcast.40), kind=kLoop, calls=%fused_computation.9 | loop fusion | flops 2097152 | bytes 8454144 | tf_op jit(solution)/shard_map/mul | solution.py:23
  12.8 0.0 all-gather.2.cloned.1.call-update
  12.9 0.0 all-reduce.2.cloned.1.call-start
  12.9 0.7 convert_bitcast_fusion.1
  13.6 2.7 mul.31
  16.3 10.4 %copy.9 = bf16[64,8,64,256]{3,1,2,0:T(8,128)(2,1)S(1)} copy(bf16[64,8,64,256]{3,2,1,0:T(8,128)(2,1)S(1)} %bitcast.39) | data formatting | bytes 33554432
  26.8 9.7 %bitcast_multiply_fusion = bf16[512,16384]{1,0:T(8,128)(2,1)S(1)} fusion(bf16[512,16384]{1,0:T(8,128)(2,1)S(1)} %bitcast.38, bf16[1,512,16384]{2,1,0:T(8,128)(2,1)} %param.5), kind=kLoop, calls=%fused_computation.6 | loop fusion | flops 8388608 | bytes 50331648 | tf_op jit(solution)/shard_map/mul | solution.py:19
  36.5 0.0 copy-start
  36.5 5.9 %copy-done = bf16[512,16384]{1,0:T(8,128)(2,1)} copy-done((bf16[512,16384]{1,0:T(8,128)(2,1)}, bf16[512,16384]{1,0:T(8,128)(2,1)S(1)}, u32[]{:S(2)}) %copy-start) | copy-done | bytes 16777240
  42.5 0.0 copy-start.2
  42.5 127.9 %all-gather.2.cloned.1.call-done = bf16[2,256,16384]{2,1,0:T(8,128)(2,1)} async-done(((bf16[2,64,16384]{2,1,0:T(8,128)(2,1)}), bf16[2,256,16384]{2,1,0:T(8,128)(2,1)}) %all-gather.2.cloned.1.call-update) | async-done | bytes 16777232 | tf_op jit(solution)/shard_map/all_gather | solution.py:29
  170.4 6.7 %slice_bitcast_fusion.1 = (bf16[256,16384]{1,0:T(8,128)(2,1)S(1)}, bf16[256,16384]{1,0:T(8,128)(2,1)S(1)}) fusion(bf16[2,256,16384]{2,1,0:T(8,128)(2,1)} %all-gather.2.cloned.1.call-done), kind=kLoop, calls=%fused_computation.8 | loop fusion | bytes 33554432 | tf_op jit(solution)/shard_map/squeeze | solution.py:32
  177.1 0.0 copy-start.1
  177.2 3.2 copy-done.1
  180.4 1.2 maximum_select_fusion
  181.6 0.0 all-reduce.2.cloned.1.call-update
  181.6 0.0 reduce-scatter.2.cloned.1.call-start
  181.7 26.6 %all-reduce.2.cloned.1.call-done = bf16[1024,512]{1,0:T(8,128)(2,1)} async-done(((bf16[1024,512]{1,0:T(8,128)(2,1)}), bf16[1024,512]{1,0:T(8,128)(2,1)}) %all-reduce.2.cloned.1.call-update) | async-done | bytes 1048592 | tf_op jit(solution)/shard_map/psum | solution.py:9
  208.3 0.0 copy-done.2
  208.3 9.3 %fusion = bf16[256,16384]{1,0:T(8,128)(2,1)} fusion(bf16[1024,512]{1,0:T(8,128)(2,1)} %all-reduce.2.cloned.1.call-done, bf16[1,2,256,256]{3,2,1,0:T(8,128)(2,1)S(1)} %copy-done.2, bf16[2,256,16384]{2,1,0:T(8,128)(2,1)} %all-gather.2.cloned.1.call-done), kind=kOutput, calls=%fused_computation.2 | convolution fusion | flops 2193686528 | bytes 25427968 | tf_op jit(solution)/shard_map/dot_general | solution.py:46
  217.6 1.2 convolution_convert_fusion.1
  218.8 1.5 convolution_convert_fusion
  220.3 22.0 %select_convert_fusion = bf16[512,16384]{1,0:T(8,128)(2,1)} fusion(bf16[512,16384]{1,0:T(8,128)(2,1)} %copy-done, bf16[256,16384]{1,0:T(8,128)(2,1)} %fusion, bf16[256,16384]{1,0:T(8,128)(2,1)} %copy-done.1, pred[16384]{0:T(1024)(128)(4,1)S(1)} %add_compare_fusion, bf16[512,256]{0,1:T(8,128)(2,1)S(1)} %convolution_convert_fusion, ...), kind=kOutput, calls=%fused_computation | convolution fusion | flops 8658092032 | bytes 50872320 | tf_op jit(solution)/shard_map/dot_general | solution.py:65
  242.2 0.0 reduce-scatter.2.cloned.1.call-update
  242.3 1.0 copy.8
  243.3 3.0 dynamic-slice_bitcast_fusion
  246.4 107.2 %reduce-scatter.2.cloned.1.call-done = bf16[32,16384]{1,0:T(8,128)(2,1)} async-done(((bf16[512,16384]{1,0:T(8,128)(2,1)}), bf16[32,16384]{1,0:T(8,128)(2,1)}) %reduce-scatter.2.cloned.1.call-update) | async-done | bytes 1048592 | tf_op jit(solution)/shard_map/reduce_scatter | solution.py:69
  353.6 2.7 bitcast_convert_fusion
  (5 shorter events, 0.1 us)
Async XLA Ops:
  7.2 163.2 %all-gather.2.cloned.1.call-start = ((), (), s32[]{:S(2)}) async-start(), calls=%async_computation.1 | async-start | bytes 20971520 | tf_op jit(solution)/shard_map/all_gather | solution.py:29
  12.9 195.4 %all-reduce.2.cloned.1.call-start = ((), (), s32[]{:S(2)}) async-start(), calls=%async_computation.2 | async-start | bytes 2097152 | tf_op jit(solution)/shard_map/psum | solution.py:9
  36.5 6.0 %copy-start = (bf16[512,16384]{1,0:T(8,128)(2,1)}, bf16[512,16384]{1,0:T(8,128)(2,1)S(1)}, u32[]{:S(2)}) copy-start(bf16[512,16384]{1,0:T(8,128)(2,1)S(1)} %bitcast_multiply_fusion) | copy-start | bytes 50331652
  42.5 165.8 %copy-start.2 = (bf16[1,2,256,256]{3,2,1,0:T(8,128)(2,1)S(1)}, bf16[1,2,256,256]{3,2,1,0:T(8,128)(2,1)}, u32[]{:S(2)}) copy-start(bf16[1,2,256,256]{3,2,1,0:T(8,128)(2,1)} %param.7) | copy-start | bytes 786436
  177.1 3.2 copy-start.1
  181.6 172.0 %reduce-scatter.2.cloned.1.call-start = ((), (), s32[]{:S(2)}) async-start(), calls=%async_computation.3 | async-start | bytes 17825792 | tf_op jit(solution)/shard_map/reduce_scatter | solution.py:69
Sparse Core Ops, SparseCore 0:
  13.0 157.3 all-gather.1
  181.7 26.5 all-reduce.1
  242.4 111.1 reduce-scatter.1
where the time goes:
time: 363 us
  waiting for transfers between devices  262 us (72%)
  matrix products  33.9 us (9%)
  local copies, waits for them, and re-layouts  33.3 us (9%)
  other arithmetic  19.8 us (5%)
  between operations  13.9 us (4%)
    all_gather x1, waiting for transfers between devices, on_device(): gathered = lax.all_gather(pivot_masked, 'prow', axis=1, tiled=True)  128 us
    reduce_scatter x1, waiting for transfers between devices, on_device(): lax.psum_scatter(schur_rows.astype(jnp.bfloat16), 'layer', scatter_dimens...  107 us
    psum x1, waiting for transfers between devices, spread(): return lax.psum(jnp.where(mine, value, jnp.zeros_like(value)), axis)  26.6 us
    dot_general x1, matrix products, on_device(): jnp.dot(lower_panel, stacked, preferred_element_type=jnp.float32)  22 us
    unnamed x10, local copies, waits for them, and re-layouts  20.7 us
    mul x1, other arithmetic, on_device(): front[0]  9.72 us
    dot_general x1, matrix products, on_device(): jnp.dot(lower_pivot, upper_first, preferred_element_type=jnp.float32)  9.25 us
  transfers between devices with their start and end apart: 3, of which 3 were waited for; matrix products, arithmetic and copies ran while one was open for 8% of the time, Pallas kernels for 0%

commit v1 on v0

--- a/solution.py
+++ b/solution.py
@@ -26,7 +26,24 @@
     first_inverse = inverses[0, 0]
     second_inverse = inverses[0, 1]
     row_offset = lax.axis_index("prow") * own_rows
-    gathered = lax.all_gather(pivot_masked, "prow", axis=1, tiled=True)
+    size, mine_2, rows = (lax.axis_size("prow"), lax.axis_index("prow"), pivot_masked.shape[1])
+    forward = [(i, (i + 1) % size) for i in range(size)]
+    downward = [(i, (i - 1) % size) for i in range(size)]
+    out = jnp.zeros(
+        (*pivot_masked.shape[:1], size * rows, *pivot_masked.shape[1 + 1 :]), pivot_masked.dtype
+    )
+    out = lax.dynamic_update_slice_in_dim(out, pivot_masked, mine_2 * rows, axis=1)
+    from_left = from_right = pivot_masked
+    middle = size // 2
+    for hop in range(1, middle + 1):
+        from_left = lax.ppermute(from_left, "prow", forward)
+        out = lax.dynamic_update_slice_in_dim(out, from_left, (mine_2 - hop) % size * rows, axis=1)
+        if hop < size - middle:
+            from_right = lax.ppermute(from_right, "prow", downward)
+            out = lax.dynamic_update_slice_in_dim(
+                out, from_right, (mine_2 + hop) % size * rows, axis=1
+            )
+    gathered = out
     panel_cols = spread(
         jnp.concatenate(
             [masked[:, :panel_width], gathered[0][:, :panel_width], gathered[1][:, :panel_width]], 0

time: 363 us -> 398 us (1.096)
  local copies, waits for them, and re-layouts: 33.3 us -> 52 us
  waiting for transfers between devices: 262 us -> 271 us
  starting transfers between devices: 0.12 us -> 4.85 us
    ppermute x0 -> x3, waiting for transfers between devices: none -> 138 us  [the longest x2 138 us: on_device(): from_left = lax.ppermute(from_left, 'prow', forward)]
    all_gather x1 -> x0, waiting for transfers between devices: 128 us -> none  [on_device(): gathered = lax.all_gather(pivot_masked, 'prow', axis=1, tiled=True)]
    dynamic_update_slice x0 -> x3, local copies, waits for them, and re-layouts: none -> 13.5 us  [the longest x2 9 us: on_device(): lax.dynamic_update_slice_in_dim(out, from_left, (mine_2 - hop) % size * r...]
    mul x1 -> x0, other arithmetic: 4.78 us -> none  [on_device(): pivots[0].reshape(2, own_rows, col_count // block_size, block_size)]
    ppermute x0 -> x3, starting transfers between devices: none -> 4.59 us  [the longest x2 2.47 us: on_device(): from_left = lax.ppermute(from_left, 'prow', forward)]
    mul x1, other arithmetic: 9.72 us -> 14 us  [on_device(): front[0]]
    unnamed x10 -> x14, local copies, waits for them, and re-layouts: 20.7 us -> 21.1 us
  transfers between devices with their start and end apart: 3 -> 5, of which waited for: 3 -> 4; matrix products, arithmetic and copies ran while one was open for 8% -> 12% of each run, Pallas kernels for 0% -> 0%
where the time goes in v1:
time: 398 us
  waiting for transfers between devices  271 us (68%)
  local copies, waits for them, and re-layouts  52 us (13%)
  matrix products  34 us (9%)
  other arithmetic  21.6 us (5%)
  between operations  14.2 us (4%)
  starting transfers between devices  4.85 us (1%)
    ppermute x2, waiting for transfers between devices, on_device(): from_left = lax.ppermute(from_left, 'prow', forward)  138 us
    reduce_scatter x1, waiting for transfers between devices, on_device(): lax.psum_scatter(schur_rows.astype(jnp.bfloat16), 'layer', scatter_dimens...  107 us
    psum x1, waiting for transfers between devices, spread(): return lax.psum(jnp.where(mine, value, jnp.zeros_like(value)), axis)  25.9 us
    dot_general x1, matrix products, on_device(): jnp.dot(lower_panel, stacked, preferred_element_type=jnp.float32)  21.9 us
    unnamed x14, local copies, waits for them, and re-layouts  21.1 us
    mul x1, other arithmetic, on_device(): front[0]  14 us
    dot_general x1, matrix products, on_device(): jnp.dot(lower_pivot, upper_first, preferred_element_type=jnp.float32)  9.32 us
    dynamic_update_slice x2, local copies, waits for them, and re-layouts, on_device(): lax.dynamic_update_slice_in_dim(out, from_left, (mine_2 - hop) % size * r...  9 us
  transfers between devices with their start and end apart: 5, of which 4 were waited for; matrix products, arithmetic and copies ran while one was open for 12% of the time, Pallas kernels for 0%

profile of v1, /device:TPU:1, one launch (start us, length us, event | category | flops | bytes accessed | tf_op | source)
XLA Modules:
  0.0 397.5 jit_solution(14270966305455092176)
XLA Ops:
  7.2 0.0 copy-start.4
  7.2 0.0 all-reduce.2.cloned.1.call-start
  7.2 0.7 convert_bitcast_fusion
  7.9 0.1 broadcast_bitcast_fusion
  8.0 0.1 copy.10
  8.1 0.0 copy-start.2
  8.1 1.2 broadcast_in_dim.27
  9.3 1.0 copy-done.2
  10.3 3.1 constant_dynamic-update-slice_fusion.3
  13.3 0.0 copy-start
  13.3 2.5 collective-permute-start
  15.8 2.1 collective-permute-start.1
  17.9 0.0 copy-done.4
  17.9 6.3 %mul.41 = bf16[2,256,64,256]{3,2,1,0:T(8,128)(2,1)} broadcast(bf16[2,64]{1,0:T(2,128)(2,1)S(1)} %convert_bitcast_fusion.1), dimensions={0,2} | broadcast | bytes 16777472 | tf_op jit(solution)/shard_map/mul | solution.py:19
  24.2 15.8 %copy.9 = bf16[64,8,64,256]{3,1,2,0:T(8,128)(2,1)S(1)} copy(bf16[64,8,64,256]{3,2,1,0:T(8,128)(2,1)} %bitcast.40) | data formatting | bytes 33554432
  40.0 0.0 copy-done
  40.0 68.5 %collective-permute-done = bf16[2,64,16384]{2,1,0:T(8,128)(2,1)} collective-permute-done((bf16[2,64,16384]{2,1,0:T(8,128)(2,1)}, bf16[2,64,16384]{2,1,0:T(8,128)(2,1)}, u32[]{:S(2)}, u32[]{:S(2)}) %collective-permute-start) | collective-permute-done | bytes 4194336 | tf_op jit(solution)/shard_map/ppermute | solution.py:39
  108.5 0.0 collective-permute-start.2
  108.5 14.0 %bitcast_multiply_fusion = bf16[512,16384]{1,0:T(8,128)(2,1)} fusion(bf16[512,16384]{1,0:T(8,128)(2,1)S(1)} %bitcast.39, bf16[1,512,16384]{2,1,0:T(8,128)(2,1)} %param.5), kind=kLoop, calls=%fused_computation.4 | loop fusion | flops 8388608 | bytes 50331648 | tf_op jit(solution)/shard_map/mul | solution.py:19
  122.5 4.5 %constant_dynamic-update-slice_fusion.2 = bf16[2,256,16384]{2,1,0:T(8,128)(2,1)} fusion(bf16[2,256,16384]{2,1,0:T(8,128)(2,1)} %copy-done, bf16[2,64,16384]{2,1,0:T(8,128)(2,1)} %collective-permute-done, s32[]{:T(128)S(6)} %select_n.43), kind=kLoop, calls=%fused_computation.35 | loop fusion | bytes 8388612 | tf_op jit(solution)/shard_map/dynamic_update_slice | solution.py:40
  127.0 0.0 collective-permute-done.1
  127.0 4.5 %constant_dynamic-update-slice_fusion.1 = bf16[2,256,16384]{2,1,0:T(8,128)(2,1)} fusion(bf16[2,256,16384]{2,1,0:T(8,128)(2,1)} %constant_dynamic-update-slice_fusion.2, bf16[2,64,16384]{2,1,0:T(8,128)(2,1)} %collective-permute-done.1, s32[]{:T(128)S(6)} %select_n.45), kind=kLoop, calls=%fused_computation.34 | loop fusion | bytes 8388612 | tf_op jit(solution)/shard_map/dynamic_update_slice | solution.py:43
  131.5 69.4 %collective-permute-done.2 = bf16[2,64,16384]{2,1,0:T(8,128)(2,1)} collective-permute-done((bf16[2,64,16384]{2,1,0:T(8,128)(2,1)}, bf16[2,64,16384]{2,1,0:T(8,128)(2,1)}, u32[]{:S(2)}, u32[]{:S(2)}) %collective-permute-start.2) | collective-permute-done | bytes 4194336 | tf_op jit(solution)/shard_map/ppermute | solution.py:39
  200.9 4.5 %constant_dynamic-update-slice_fusion = bf16[2,256,16384]{2,1,0:T(8,128)(2,1)} fusion(bf16[2,256,16384]{2,1,0:T(8,128)(2,1)} %constant_dynamic-update-slice_fusion.1, bf16[2,64,16384]{2,1,0:T(8,128)(2,1)} %collective-permute-done.2, s32[]{:T(128)S(6)} %select_n.47), kind=kLoop, calls=%fused_computation.33 | loop fusion | bytes 8388612 | tf_op jit(solution)/shard_map/dynamic_update_slice | solution.py:40
  205.4 0.0 slice-start
  205.4 0.0 copy-start.3
  205.4 6.8 %slice_bitcast_fusion.1 = (bf16[256,16384]{1,0:T(8,128)(2,1)S(1)}, bf16[256,16384]{1,0:T(8,128)(2,1)S(1)}) fusion(bf16[2,256,16384]{2,1,0:T(8,128)(2,1)} %constant_dynamic-update-slice_fusion), kind=kLoop, calls=%fused_computation.7 | loop fusion | bytes 33554432 | tf_op jit(solution)/shard_map/squeeze | solution.py:49
  212.2 0.0 copy-start.1
  212.3 3.2 copy-done.1
  215.5 0.0 slice-done
  215.5 1.2 maximum_select_fusion
  216.7 0.0 all-reduce.2.cloned.1.call-update
  216.7 0.2 reduce-scatter.2.cloned.1.call-start
  216.9 25.9 %all-reduce.2.cloned.1.call-done = bf16[1024,512]{1,0:T(8,128)(2,1)} async-done(((bf16[1024,512]{1,0:T(8,128)(2,1)}), bf16[1024,512]{1,0:T(8,128)(2,1)}) %all-reduce.2.cloned.1.call-update) | async-done | bytes 1048592 | tf_op jit(solution)/shard_map/psum | solution.py:9
  242.8 0.0 copy-done.3
  242.8 9.3 %subtract_convert_fusion = bf16[256,16384]{1,0:T(8,128)(2,1)} fusion(bf16[1024,512]{1,0:T(8,128)(2,1)} %all-reduce.2.cloned.1.call-done, bf16[1,2,256,256]{3,2,1,0:T(8,128)(2,1)S(1)} %copy-done.3, bf16[2,256,16384]{2,1,0:T(8,128)(2,1)} %constant_dynamic-update-slice_fusion), kind=kOutput, calls=%fused_computation.5 | convolution fusion | flops 2193686528 | bytes 25427968 | tf_op jit(solution)/shard_map/dot_general | solution.py:63
  252.1 1.2 convolution_convert_fusion.1
  253.4 1.5 convolution_convert_fusion
  254.9 21.9 %select_convert_fusion = bf16[512,16384]{1,0:T(8,128)(2,1)} fusion(bf16[512,16384]{1,0:T(8,128)(2,1)} %bitcast_multiply_fusion, bf16[256,16384]{1,0:T(8,128)(2,1)} %subtract_convert_fusion, bf16[256,16384]{1,0:T(8,128)(2,1)} %copy-done.1, pred[16384]{0:T(1024)(128)(4,1)S(1)} %add_compare_fusion, bf16[512,256]{0,1:T(8,128)(2,1)S(1)} %convolution_convert_fusion, ...), kind=kOutput, calls=%fused_computation | convolution fusion | flops 8658092032 | bytes 50872320 | tf_op jit(solution)/shard_map/dot_general | solution.py:82
  276.8 0.0 reduce-scatter.2.cloned.1.call-update
  276.9 1.0 copy.8
  277.9 3.0 dynamic-slice_bitcast_fusion
  280.9 107.1 %reduce-scatter.2.cloned.1.call-done = bf16[32,16384]{1,0:T(8,128)(2,1)} async-done(((bf16[512,16384]{1,0:T(8,128)(2,1)}), bf16[32,16384]{1,0:T(8,128)(2,1)}) %reduce-scatter.2.cloned.1.call-update) | async-done | bytes 1048592 | tf_op jit(solution)/shard_map/reduce_scatter | solution.py:86
  388.0 2.7 bitcast_convert_fusion
  (5 shorter events, 0.1 us)
Async XLA Ops:
  7.2 10.8 %copy-start.4 = (s32[1,2,64]{2,1,0:T(2,128)S(1)}, s32[1,2,64]{2,1,0:T(2,128)}, u32[]{:S(2)}) copy-start(s32[1,2,64]{2,1,0:T(2,128)} %param.8) | copy-start | bytes 1540
  7.2 235.6 %all-reduce.2.cloned.1.call-start = ((), (), s32[]{:S(2)}) async-start(), calls=%async_computation.1 | async-start | bytes 2097152 | tf_op jit(solution)/shard_map/psum | solution.py:9
  8.1 2.2 copy-start.2
  13.3 26.7 %copy-start = (bf16[2,256,16384]{2,1,0:T(8,128)(2,1)}, bf16[2,256,16384]{2,1,0:T(8,128)(2,1)S(1)}, u32[]{:S(2)}) copy-start(bf16[2,256,16384]{2,1,0:T(8,128)(2,1)S(1)} %get-tuple-element.6) | copy-start | bytes 50331652
  13.3 95.2 %collective-permute-start = (bf16[2,64,16384]{2,1,0:T(8,128)(2,1)}, bf16[2,64,16384]{2,1,0:T(8,128)(2,1)}, u32[]{:S(2)}, u32[]{:S(2)}) collective-permute-start(bf16[2,64,16384]{2,1,0:T(8,128)(2,1)} %get-tuple-element.7), channel_id=1, source_target_pairs={{0,2},{2,4},{4,6},{6,0},{1,3},{3,5},{5,7},{7,1},{8,10},{10,12},{12... | collective-permute-start | bytes 12582920 | tf_op jit(solution)/shard_map/ppermute | solution.py:39
  15.8 111.2 %collective-permute-start.1 = (bf16[2,64,16384]{2,1,0:T(8,128)(2,1)}, bf16[2,64,16384]{2,1,0:T(8,128)(2,1)}, u32[]{:S(2)}, u32[]{:S(2)}) collective-permute-start(bf16[2,64,16384]{2,1,0:T(8,128)(2,1)} %get-tuple-element.7), channel_id=1, source_target_pairs={{0,6},{2,0},{4,2},{6,4},{1,7},{3,1},{5,3},{7,5},{8,14},{10,8},{12,... | collective-permute-start | bytes 12582920 | tf_op jit(solution)/shard_map/ppermute | solution.py:42
  108.5 92.4 %collective-permute-start.2 = (bf16[2,64,16384]{2,1,0:T(8,128)(2,1)}, bf16[2,64,16384]{2,1,0:T(8,128)(2,1)}, u32[]{:S(2)}, u32[]{:S(2)}) collective-permute-start(bf16[2,64,16384]{2,1,0:T(8,128)(2,1)} %collective-permute-done), channel_id=1, source_target_pairs={{0,2},{2,4},{4,6},{6,0},{1,3},{3,5},{5,7},{7,1},{8,10},{10,12},{12... | collective-permute-start | bytes 12582920 | tf_op jit(solution)/shard_map/ppermute | solution.py:39
  205.4 10.1 %slice-start = ((bf16[512,16384]{1,0:T(8,128)(2,1)}), bf16[512,512]{1,0:T(8,128)(2,1)S(1)}, s32[]{:S(2)}) async-start(bf16[512,16384]{1,0:T(8,128)(2,1)} %bitcast_multiply_fusion), calls=%async_computation.3 | async-start | bytes 1048576 | tf_op jit(solution)/shard_map/slice | solution.py:49
  205.4 37.4 %copy-start.3 = (bf16[1,2,256,256]{3,2,1,0:T(8,128)(2,1)S(1)}, bf16[1,2,256,256]{3,2,1,0:T(8,128)(2,1)}, u32[]{:S(2)}) copy-start(bf16[1,2,256,256]{3,2,1,0:T(8,128)(2,1)} %param.7) | copy-start | bytes 786436
  212.2 3.2 copy-start.1
  216.7 171.3 %reduce-scatter.2.cloned.1.call-start = ((), (), s32[]{:S(2)}) async-start(), calls=%async_computation.2 | async-start | bytes 17825792 | tf_op jit(solution)/shard_map/reduce_scatter | solution.py:86
Sparse Core Ops, SparseCore 0:
  216.8 25.9 all-reduce.1
  276.9 111.0 reduce-scatter.1
